TPU v7x, 32 devices: a whole 2x2x4 slice. The times are simulated.
32 devices in a mesh: groups: 2 (over y), rows: 8 (over z, x), heads: 2 (over core).
Axes of the slice: x: 2, y: 2, z: 4, core: 2. Of those that a mesh axis runs over, the one named last changes fastest.
Arguments:
- residual_in: bfloat16 [128, 8192], P(('groups', 'rows'), 'heads'), parts along dimension 0, may hold values from -6 to 6
- query: bfloat16 [128, 8192], P(('groups', 'rows'), 'heads'), parts along dimension 0, may hold values from -120 to 120
- key_cache: bfloat16 [128, 4, 32, 128], P(('groups', 'rows'), 'heads'), parts along dimension 0, may hold values from -4 to 4
- value_cache: bfloat16 [128, 4, 32, 128], P(('groups', 'rows'), 'heads'), parts along dimension 0, may hold values from -5 to 5
- key_new: bfloat16 [128, 4, 128], P(('groups', 'rows'), 'heads'), parts along dimension 0, may hold values from -4 to 4
- value_new: bfloat16 [128, 4, 128], P(('groups', 'rows'), 'heads'), parts along dimension 0, may hold values from -5 to 5
- lengths: int32 [128], P(('groups', 'rows')), parts along dimension 0, may hold values from 2 to 32, as said below
- norm_gain: bfloat16 [8192], replicated, may hold values from 0.3984375 to 1.59375
- hot_gate: bfloat16 [128, 8192], P('heads'), may hold values from -0.0625 to 0.0625
- hot_up: bfloat16 [128, 8192], P('heads'), may hold values from -0.0625 to 0.0625
- hot_down: bfloat16 [128, 8192], P('heads'), may hold values from -0.5 to 0.5
- cold_gate: bfloat16 [512, 8192], P(('rows', 'heads')), may hold values from -0.0625 to 0.0625
- cold_up: bfloat16 [512, 8192], P(('rows', 'heads')), may hold values from -0.0625 to 0.0625
- cold_down: bfloat16 [512, 8192], P(('rows', 'heads')), may hold values from -0.5 to 0.5
- active: int32 [128, 4], P(('groups', 'rows')), parts along dimension 0, may hold values from 0 to 1, as said below
Outputs:
- residual_out: bfloat16 [128, 8192], P(('groups', 'rows'), 'heads'), parts along dimension 0
There are 2 independent parts, one for each index of `groups`. A program takes and returns all parts, laid end to end along the dimension named above; an argument that names none is the same for every part. Nothing has to cross between parts.
Inputs may be any that keep to these rules, and one draw needn't show every extreme that they name: `lengths`: every request has at least two filled slots, and some request has all 32. `active`: 0 or 1; among the 8 requests of one index of rows at most 2 are active on any one cold block, and exactly 2 on some.
All inputs are finite; a program needn't handle non-finite values.
Results may differ from a plain program's by a relative error of at most 0.0085.
Values may be sent and summed in bfloat16 or wider, within the bound.
No kernel may reach another device: no remote copies, remote signals or barrier semaphores. Data moves between devices by JAX's collectives and lax.ppermute only.
A program may use at most 64 MiB of HBM per device.

v0:
```python
import jax
import jax.numpy as jnp
from jax import lax
from jax.sharding import PartitionSpec as P

HD = 128
D = 8192
CAP = 2


def partner(block, axis, bit):
    count = lax.axis_size(axis)
    route = []
    for low in range(count):
        high = low | 1 << bit
        if high != low and high < count:
            route += [(low, high), (high, low)]
    return lax.ppermute(block, axis, route)


def join_halves(half, myself):
    other = partner(half, "heads", 0)
    low_first = jnp.concatenate([half, other], axis=1)
    high_first = jnp.concatenate([other, half], axis=1)
    return jnp.where(myself == 0, low_first, high_first)


def attention_rows(query, key_cache, value_cache, key_new, value_new, lengths):
    count = key_cache.shape[0]
    kv_local = key_cache.shape[1]
    scale_factor = 1.0 / HD**0.5
    queries = query.reshape(count, kv_local, -1, HD)
    scores = (
        jnp.einsum("rgjd,rgpd->rgjp", queries, key_cache, preferred_element_type=jnp.float32)
        * scale_factor
    )
    own_score = (
        jnp.einsum("rgjd,rgd->rgj", queries, key_new, preferred_element_type=jnp.float32)
        * scale_factor
    )
    visible = (jnp.arange(key_cache.shape[2], dtype=jnp.int32)[None, :] < lengths[:, None])[
        :, None, None, :
    ]
    scores = jnp.where(visible, scores, -1e30)
    highest = jnp.maximum(jnp.max(scores, axis=-1), own_score)
    expons = jnp.where(visible, jnp.exp(scores - highest[..., None]), 0.0)
    own_expon = jnp.exp(own_score - highest)
    totals = jnp.sum(expons, axis=-1) + own_expon
    weights = (expons / totals[..., None]).astype(jnp.bfloat16)
    own_weight = (own_expon / totals).astype(jnp.bfloat16)
    blended = jnp.einsum(
        "rgjp,rgpd->rgjd", weights, value_cache, preferred_element_type=jnp.float32
    )
    blended = (
        blended
        + own_weight.astype(jnp.float32)[..., None] * value_new.astype(jnp.float32)[:, :, None, :]
    )
    return blended.reshape(count, -1)


def swiglu_rows(normed, gate_rows, up_rows, down_rows):
    gate = jnp.einsum("rd,nd->rn", normed, gate_rows, preferred_element_type=jnp.float32)
    upper = jnp.einsum("rd,nd->rn", normed, up_rows, preferred_element_type=jnp.float32)
    hidden = (jax.nn.silu(gate) * upper).astype(jnp.bfloat16)
    return jnp.dot(hidden, down_rows, preferred_element_type=jnp.float32)


def collect_rows(selector, returned):
    return lax.dot_general(
        selector,
        returned,
        (((0,), (0,)), ((), ())),
        precision=lax.Precision.HIGHEST,
        preferred_element_type=jnp.float32,
    )


def local(
    residual_in,
    query,
    key_cache,
    value_cache,
    key_new,
    value_new,
    lengths,
    norm_gain,
    hot_gate,
    hot_up,
    hot_down,
    cold_gate,
    cold_up,
    cold_down,
    active,
):
    attended = attention_rows(query, key_cache, value_cache, key_new, value_new, lengths)
    stream = (residual_in.astype(jnp.float32) + attended).astype(jnp.bfloat16)
    half_width = stream.shape[1]
    myself = lax.axis_index("heads")
    local_wide = stream.astype(jnp.float32)
    square_part = jnp.sum(local_wide * local_wide, axis=-1)
    square_total = square_part + partner(square_part, "heads", 0)
    gain_half = lax.dynamic_slice_in_dim(norm_gain, myself * half_width, half_width)
    scaled = (
        local_wide * lax.rsqrt(square_total / D + 1e-05)[:, None] * gain_half.astype(jnp.float32)
    )
    normed = join_halves(scaled.astype(jnp.bfloat16), myself)
    hot_part = swiglu_rows(normed, hot_gate, hot_up, hot_down)
    owner_count = lax.axis_size("rows")
    block_count = active.shape[1]
    request_count = active.shape[0]
    by_block = jnp.transpose(active)
    earlier = jnp.cumsum(by_block, axis=1) - by_block
    slot_ids = jnp.arange(CAP, dtype=jnp.int32)[None, :, None]
    slot_table = by_block[:, None, :] * (earlier[:, None, :] == slot_ids).astype(jnp.int32)
    selector = jnp.repeat(slot_table, owner_count // block_count, axis=0).reshape(
        owner_count * CAP, request_count
    )
    outgoing = jnp.dot(
        selector.astype(jnp.bfloat16), normed, preferred_element_type=jnp.float32
    ).astype(jnp.bfloat16)
    incoming = lax.all_to_all(outgoing, "rows", split_axis=0, concat_axis=0, tiled=True)
    cold_part = swiglu_rows(incoming, cold_gate, cold_up, cold_down)
    selector_wide = selector.astype(jnp.float32)
    kept = lax.dynamic_slice_in_dim(cold_part, myself * half_width, half_width, 1)
    given = lax.dynamic_slice_in_dim(cold_part, (1 - myself) * half_width, half_width, 1)
    owner_sum = kept + partner(given, "heads", 0)
    returned = lax.all_to_all(owner_sum, "rows", split_axis=0, concat_axis=0, tiled=True)
    cold_sum = collect_rows(selector_wide, returned)
    hot_kept = lax.dynamic_slice_in_dim(hot_part, myself * half_width, half_width, 1)
    hot_given = lax.dynamic_slice_in_dim(hot_part, (1 - myself) * half_width, half_width, 1)
    hot_total = hot_kept + partner(hot_given, "heads", 0)
    result = stream.astype(jnp.float32) + hot_total + cold_sum
    return result.astype(jnp.bfloat16)


def solution(mesh):
    return jax.shard_map(
        local,
        mesh=mesh,
        in_specs=(
            P(("groups", "rows"), "heads"),
            P(("groups", "rows"), "heads"),
            P(("groups", "rows"), "heads", None, None),
            P(("groups", "rows"), "heads", None, None),
            P(("groups", "rows"), "heads", None),
            P(("groups", "rows"), "heads", None),
            P(("groups", "rows")),
            P(),
            P("heads", None),
            P("heads", None),
            P("heads", None),
            P(("rows", "heads"), None),
            P(("rows", "heads"), None),
            P(("rows", "heads"), None),
            P(("groups", "rows"), None),
        ),
        out_specs=P(("groups", "rows"), "heads"),
        check_vma=False,
    )
```

profile of v0, /device:TPU:0, one launch (start us, length us, event | category | flops | bytes accessed | tf_op | source)
XLA Modules:
  0.0 45.1 jit_solution(7972570449464875627)
XLA Ops:
  0.0 0.8 %iota_compare_fusion = pred[8,32]{1,0:T(8,128)(4,1)S(1)} fusion(s32[8]{0:T(128)} %param.21), kind=kLoop, calls=%fused_computation.44 | loop fusion | flops 256 | bytes 288 | tf_op jit(solution)/shard_map/lt | solution.py:41
  0.8 1.0 %fusion.14 = f32[8,2,1,16]{3,2,1,0:T(1,128)S(1)} fusion(bf16[8,2,16,128]{3,0,2,1:T(8,128)(2,1)} %bitcast.29, bf16[8,2,128,1]{2,1,0,3:T(2,128)(2,1)} %bitcast.37), kind=kOutput, calls=%fused_computation.26 | convolution fusion | flops 65536 | bytes 70656 | tf_op jit(solution)/shard_map/rgjd,rgd->rgj/dot_general | solution.py:38
  1.8 1.2 %fusion.36 = (f32[8,2,16]{2,1,0:T(2,128)S(1)}, f32[8,2,16,32]{3,2,1,0:T(8,128)S(1)}) fusion(bf16[8,2,32,128]{3,2,1,0:T(8,128)(2,1)} %param.17, bf16[8,2,16,128]{3,0,2,1:T(8,128)(2,1)S(1)} %bitcast.30, pred[8,32]{1,0:T(8,128)(4,1)S(1)} %iota_compare_fusion), kind=kOutput, calls=%fused_computation.58 | convolution fusion | flops 2121472 | bytes 230656 | tf_op jit(solution)/shard_map/rgjd,rgpd->rgjp/dot_general | solution.py:34
  3.0 0.2 fusion.9
  3.3 0.7 %copy-done.8 = bf16[8,2,128]{2,1,0:T(2,128)(2,1)S(1)} copy-done((bf16[8,2,128]{2,1,0:T(2,128)(2,1)S(1)}, bf16[8,2,128]{2,1,0:T(2,128)(2,1)}, u32[]{:S(2)}) %copy-start.8) | copy-done | bytes 4120
  4.0 0.3 convolution_add_fusion
  4.2 0.5 %copy-done.5 = bf16[8,4096]{1,0:T(8,128)(2,1)S(1)} copy-done((bf16[8,4096]{1,0:T(8,128)(2,1)S(1)}, bf16[8,4096]{1,0:T(8,128)(2,1)}, u32[]{:S(2)}) %copy-start.5) | copy-done | bytes 65560
  4.8 0.2 fusion.3
  5.0 0.5 %collective-permute-start = (f32[8]{0:T(128)S(1)}, f32[8]{0:T(128)S(1)}, u32[]{:S(2)}, u32[]{:S(2)}) collective-permute-start(f32[8]{0:T(128)S(1)} %get-tuple-element.5), channel_id=1, source_target_pairs={{0,1},{1,0},{2,3},{3,2},{4,5},{5,4},{6,7},{7,6},{8,9},{9,8},{10,11... | collective-permute-start | bytes 104 | tf_op jit(solution)/shard_map/ppermute | solution.py:18
  5.5 0.2 reduce_window_sum.11
  5.7 0.6 %collective-permute-done = f32[8]{0:T(128)S(1)} collective-permute-done((f32[8]{0:T(128)S(1)}, f32[8]{0:T(128)S(1)}, u32[]{:S(2)}, u32[]{:S(2)}) %collective-permute-start) | collective-permute-done | bytes 64 | tf_op jit(solution)/shard_map/ppermute | solution.py:18
  6.3 0.1 fusion.5
  6.4 0.4 collective-permute-start.1
  6.8 0.9 %collective-permute-done.1 = bf16[8,4096]{1,0:T(8,128)(2,1)S(1)} collective-permute-done((bf16[8,4096]{1,0:T(8,128)(2,1)S(1)}, bf16[8,4096]{1,0:T(8,128)(2,1)S(1)}, u32[]{:S(2)}, u32[]{:S(2)}) %collective-permute-start.1) | collective-permute-done | bytes 65568 | tf_op jit(solution)/shard_map/ppermute | solution.py:18
  7.7 0.2 convolution_convert_fusion
  8.0 0.9 %all_to_all.16 = bf16[8,2,8192]{2,1,0:T(2,128)(2,1)} reshape(bf16[16,8192]{1,0:T(8,128)(2,1)S(1)} %convolution_convert_fusion) | data formatting | bytes 524288 | tf_op jit(solution)/shard_map/all_to_all | solution.py:121
  8.9 7.1 %all-to-all-start = ((bf16[8,2,8192]{2,1,0:T(2,128)(2,1)}), bf16[8,2,8192]{2,1,0:T(2,128)(2,1)S(1)}, u32[]{:S(2)}, u32[]{:S(2)}) async-start(bf16[8,2,8192]{2,1,0:T(2,128)(2,1)} %all_to_all.16), calls=%async_computation | async-start | bytes 524288 | tf_op jit(solution)/shard_map/all_to_all | solution.py:121
  16.0 0.4 fusion.33
  16.3 8.9 %all-to-all-done = bf16[8,2,8192]{2,1,0:T(2,128)(2,1)S(1)} async-done(((bf16[8,2,8192]{2,1,0:T(2,128)(2,1)}), bf16[8,2,8192]{2,1,0:T(2,128)(2,1)S(1)}, u32[]{:S(2)}, u32[]{:S(2)}) %all-to-all-start) | async-done | bytes 262176 | tf_op jit(solution)/shard_map/all_to_all | solution.py:121
  25.3 0.1 all_to_all.18
  25.4 0.2 fusion.37
  25.6 1.9 %fusion.2 = f32[16,8192]{1,0:T(8,128)S(1)} fusion(bf16[32,8192]{1,0:T(8,128)(2,1)} %param.28, bf16[16,8192]{1,0:T(8,128)(2,1)S(1)} %all_to_all.18, bf16[32,8192]{1,0:T(8,128)(2,1)} %param.27, f32[16,32]{1,0:T(8,128)S(1)} %fusion.37), kind=kOutput, calls=%fused_computation.6 | convolution fusion | flops 16780288 | bytes 1837056 | tf_op jit(solution)/shard_map/dot_general | solution.py:65
  27.5 0.1 collective-permute-start.3
  27.6 0.9 %fusion.27 = f32[8,8192]{1,0:T(8,128)S(1)} fusion(bf16[64,8192]{1,0:T(8,128)(2,1)S(1)} %copy-done, f32[8,64]{1,0:T(8,128)S(1)} %fusion.33, bf16[64,8192]{1,0:T(8,128)(2,1)S(1)} %copy-done.2, bf16[8,4096]{1,0:T(8,128)(2,1)S(1)} %collective-permute-done.1, bf16[8,4096]{1,0:T(8,128)(2,1)S(1)} %fusion.5, pred[]{:T(512)S(6)} %eq.16), kind=kOutput, calls=%fused_computation.46 | convolution fusion | flops 17370112 | bytes 2492417 | tf_op jit(solution)/shard_map/dot_general | solution.py:65
  28.5 0.7 %collective-permute-done.3 = f32[16,4096]{1,0:T(8,128)} collective-permute-done((f32[16,4096]{1,0:T(8,128)S(1)}, f32[16,4096]{1,0:T(8,128)}, u32[]{:S(2)}, u32[]{:S(2)}) %collective-permute-start.3) | collective-permute-done | bytes 262176 | tf_op jit(solution)/shard_map/ppermute | solution.py:18
  29.3 1.0 %dynamic-slice_add_fusion = f32[16,4096]{1,0:T(8,128)S(1)} fusion(f32[16,4096]{1,0:T(8,128)} %collective-permute-done.3, f32[16,8192]{1,0:T(8,128)S(1)} %fusion.2, s32[]{:T(128)S(6)} %select_n.27), kind=kLoop, calls=%fused_computation.7 | loop fusion | flops 65536 | bytes 786436 | tf_op jit(solution)/shard_map/add | solution.py:126
  30.2 0.9 %all_to_all.19 = f32[8,2,4096]{2,1,0:T(2,128)} reshape(f32[16,4096]{1,0:T(8,128)S(1)} %dynamic-slice_add_fusion) | data formatting | bytes 524288 | tf_op jit(solution)/shard_map/all_to_all | solution.py:127
  31.1 3.6 %all-to-all-start.1 = ((f32[8,2,4096]{2,1,0:T(2,128)}), f32[8,2,4096]{2,1,0:T(2,128)S(1)}, u32[]{:S(2)}, u32[]{:S(2)}) async-start(f32[8,2,4096]{2,1,0:T(2,128)} %all_to_all.19), calls=%async_computation.1 | async-start | bytes 524288 | tf_op jit(solution)/shard_map/all_to_all | solution.py:127
  34.7 0.1 collective-permute-start.2
  34.8 9.2 %all-to-all-done.1 = f32[8,2,4096]{2,1,0:T(2,128)S(1)} async-done(((f32[8,2,4096]{2,1,0:T(2,128)}), f32[8,2,4096]{2,1,0:T(2,128)S(1)}, u32[]{:S(2)}, u32[]{:S(2)}) %all-to-all-start.1) | async-done | bytes 262176 | tf_op jit(solution)/shard_map/all_to_all | solution.py:127
  44.0 0.2 all_to_all.21
  44.2 1.0 %fusion.7 = bf16[8,4096]{1,0:T(8,128)(2,1)} fusion(bf16[8,4096]{1,0:T(8,128)(2,1)S(1)} %get-tuple-element.6, f32[8,4096]{1,0:T(8,128)S(1)} %collective-permute-done.2, f32[8,8192]{1,0:T(8,128)S(1)} %fusion.27, s32[]{:T(128)S(6)} %select_n.27, f32[16,8]{1,0:T(8,128)S(1)} %bitcast.31, f32[16,4096]{1,0:T(8,128)S(1)} %all_to_all.21), kind=kOutput, calls=%fused_computation.15 | convolution fusion | flops 6455296 | bytes 655876 | tf_op jit(solution)/shard_map/dot_general | solution.py:69
  (30 shorter events, 0.2 us)
Async XLA Ops:
  0.0 27.6 %copy-start = (bf16[64,8192]{1,0:T(8,128)(2,1)S(1)}, bf16[64,8192]{1,0:T(8,128)(2,1)}, u32[]{:S(2)}) copy-start(bf16[64,8192]{1,0:T(8,128)(2,1)} %param.25) | copy-start | bytes 3145732
  0.0 1.8 %copy-start.4 = (bf16[8,4096]{1,0:T(8,128)(2,1)S(1)}, bf16[8,4096]{1,0:T(8,128)(2,1)}, u32[]{:S(2)}) copy-start(bf16[8,4096]{1,0:T(8,128)(2,1)} %param.16) | copy-start | bytes 196612
  3.0 1.0 %copy-start.9 = (bf16[8,2,32,128]{3,2,1,0:T(8,128)(2,1)S(1)}, bf16[8,2,32,128]{3,2,1,0:T(8,128)(2,1)}, u32[]{:S(2)}) copy-start(bf16[8,2,32,128]{3,2,1,0:T(8,128)(2,1)} %param.18) | copy-start | bytes 393220
  3.3 0.7 %copy-start.8 = (bf16[8,2,128]{2,1,0:T(2,128)(2,1)S(1)}, bf16[8,2,128]{2,1,0:T(2,128)(2,1)}, u32[]{:S(2)}) copy-start(bf16[8,2,128]{2,1,0:T(2,128)(2,1)} %param.20) | copy-start | bytes 12292
  4.0 0.8 %copy-start.5 = (bf16[8,4096]{1,0:T(8,128)(2,1)S(1)}, bf16[8,4096]{1,0:T(8,128)(2,1)}, u32[]{:S(2)}) copy-start(bf16[8,4096]{1,0:T(8,128)(2,1)} %param.15) | copy-start | bytes 196612
  4.0 1.5 %copy-start.6 = (s32[8,4]{0,1:T(4,128)S(1)}, s32[8,4]{0,1:T(4,128)}, u32[]{:S(2)}) copy-start(s32[8,4]{0,1:T(4,128)} %param.29) | copy-start | bytes 388
  4.2 1.5 %copy-start.7 = (bf16[8192]{0:T(1024)(128)(2,1)S(1)}, bf16[8192]{0:T(1024)(128)(2,1)}, u32[]{:S(2)}) copy-start(bf16[8192]{0:T(1024)(128)(2,1)} %param.22) | copy-start | bytes 49156
  4.8 11.2 %copy-start.1 = (bf16[64,8192]{1,0:T(8,128)(2,1)S(1)}, bf16[64,8192]{1,0:T(8,128)(2,1)}, u32[]{:S(2)}) copy-start(bf16[64,8192]{1,0:T(8,128)(2,1)} %param.24) | copy-start | bytes 3145732
  5.0 1.3 %collective-permute-start = (f32[8]{0:T(128)S(1)}, f32[8]{0:T(128)S(1)}, u32[]{:S(2)}, u32[]{:S(2)}) collective-permute-start(f32[8]{0:T(128)S(1)} %get-tuple-element.5), channel_id=1, source_target_pairs={{0,1},{1,0},{2,3},{3,2},{4,5},{5,4},{6,7},{7,6},{8,9},{9,8},{10,11... | collective-permute-start | bytes 104 | tf_op jit(solution)/shard_map/ppermute | solution.py:18
  6.4 1.3 %collective-permute-start.1 = (bf16[8,4096]{1,0:T(8,128)(2,1)S(1)}, bf16[8,4096]{1,0:T(8,128)(2,1)S(1)}, u32[]{:S(2)}, u32[]{:S(2)}) collective-permute-start(bf16[8,4096]{1,0:T(8,128)(2,1)S(1)} %fusion.5), channel_id=1, source_target_pairs={{0,1},{1,0},{2,3},{3,2},{4,5},{5,4},{6,7},{7,6},{8,9},{9,8},{10,11... | collective-permute-start | bytes 196616 | tf_op jit(solution)/shard_map/ppermute | solution.py:18
  8.9 16.4 %all-to-all-start = ((bf16[8,2,8192]{2,1,0:T(2,128)(2,1)}), bf16[8,2,8192]{2,1,0:T(2,128)(2,1)S(1)}, u32[]{:S(2)}, u32[]{:S(2)}) async-start(bf16[8,2,8192]{2,1,0:T(2,128)(2,1)} %all_to_all.16), calls=%async_computation | async-start | bytes 524288 | tf_op jit(solution)/shard_map/all_to_all | solution.py:121
  16.3 9.0 %copy-start.3 = (bf16[32,8192]{1,0:T(8,128)(2,1)S(1)}, bf16[32,8192]{1,0:T(8,128)(2,1)}, u32[]{:S(2)}) copy-start(bf16[32,8192]{1,0:T(8,128)(2,1)} %param.26) | copy-start | bytes 1572868
  25.6 2.0 %copy-start.2 = (bf16[64,8192]{1,0:T(8,128)(2,1)S(1)}, bf16[64,8192]{1,0:T(8,128)(2,1)}, u32[]{:S(2)}) copy-start(bf16[64,8192]{1,0:T(8,128)(2,1)} %param.23) | copy-start | bytes 3145732
  27.5 1.7 %collective-permute-start.3 = (f32[16,4096]{1,0:T(8,128)S(1)}, f32[16,4096]{1,0:T(8,128)}, u32[]{:S(2)}, u32[]{:S(2)}) collective-permute-start(f32[16,4096]{1,0:T(8,128)S(1)} %constant_dynamic-slice_fusion), channel_id=1, source_target_pairs={{0,1},{1,0},{2,3},{3,2},{4,5},{5,4},{6,7},{7,6},{8,9},{9,8},{10,11... | collective-permute-start | bytes 786440 | tf_op jit(solution)/shard_map/ppermute | solution.py:18
  31.1 12.9 %all-to-all-start.1 = ((f32[8,2,4096]{2,1,0:T(2,128)}), f32[8,2,4096]{2,1,0:T(2,128)S(1)}, u32[]{:S(2)}, u32[]{:S(2)}) async-start(f32[8,2,4096]{2,1,0:T(2,128)} %all_to_all.19), calls=%async_computation.1 | async-start | bytes 524288 | tf_op jit(solution)/shard_map/all_to_all | solution.py:127
  34.7 9.4 %collective-permute-start.2 = (f32[8,4096]{1,0:T(8,128)S(1)}, f32[8,4096]{1,0:T(8,128)S(1)}, u32[]{:S(2)}, u32[]{:S(2)}) collective-permute-start(f32[8,4096]{1,0:T(8,128)S(1)} %constant_dynamic-slice_fusion.1), channel_id=1, source_target_pairs={{0,1},{1,0},{2,3},{3,2},{4,5},{5,4},{6,7},{7,6},{8,9},{9,8},{10,11... | collective-permute-start | bytes 393224 | tf_op jit(solution)/shard_map/ppermute | solution.py:18
where the time goes:
time: 45.6 us; the launch traced here: 45.1 us
  waiting for transfers between devices  20.4 us (45%)
  starting transfers between devices  11.7 us (26%)
  matrix products  6.98 us (15%)
  local copies, waits for them, and re-layouts  3.33 us (7%)
  other arithmetic  2.53 us (6%)
    all_to_all x1, waiting for transfers between devices, local(): lax.all_to_all(owner_sum, 'rows', split_axis=0, concat_axis=0, tiled=True)  9.17 us
    all_to_all x1, waiting for transfers between devices, local(): lax.all_to_all(outgoing, 'rows', split_axis=0, concat_axis=0, tiled=True)  8.91 us
    all_to_all x1, starting transfers between devices, local(): lax.all_to_all(outgoing, 'rows', split_axis=0, concat_axis=0, tiled=True)  7.1 us
    all_to_all x1, starting transfers between devices, local(): lax.all_to_all(owner_sum, 'rows', split_axis=0, concat_axis=0, tiled=True)  3.59 us
    dot_general x2, matrix products, swiglu_rows(): return jnp.dot(hidden, down_rows, preferred_element_type=jnp.float32)  2.78 us
    ppermute x4, waiting for transfers between devices, partner(): return lax.ppermute(block, axis, route)  2.3 us
    unnamed x20, local copies, waits for them, and re-layouts  1.24 us
    dot_general x1, matrix products, attention_rows(): jnp.einsum('rgjd,rgpd->rgjp', queries, key_cache, preferred_element_type=...  1.17 us
  transfers between devices with their start and end apart: 6, of which 5 were waited for; matrix products, arithmetic and copies ran while one was open for 3% of the time, Pallas kernels for 0%

commit v1 on v0

--- a/solution.py
+++ b/solution.py
@@ -6,6 +6,44 @@
 HD = 128
 D = 8192
 CAP = 2
+
+
+def _begin_panels(load, join_dim, state):
+    w1 = load.shape
+    t_next = load.reshape(*w1[:join_dim], state, w1[join_dim] // state, *w1[join_dim + 1 :])
+    y1 = jnp.moveaxis(t_next, join_dim, 0)
+    return y1
+
+
+def get_links_by_axis(frame, d_out):
+    frame = jnp.moveaxis(frame, 0, d_out)
+    tile_out = frame.shape
+    answer = frame.reshape(
+        *tile_out[:d_out], tile_out[d_out] * tile_out[d_out + 1], *tile_out[d_out + 2 :]
+    )
+    return answer
+
+
+def convert_modes_all(axis_id, view, x0, mine_x):
+    y = lax.axis_index(axis_id)
+    state_now = lax.axis_size(axis_id)
+    q_next, local_out = (state_now, y)
+    v_now = _begin_panels(x0, mine_x, q_next)
+    value_now = v_now
+    k0 = 1
+    while k0 < q_next:
+        b_now, carry_out = ((local_out + k0) % q_next, (local_out - k0) % q_next)
+        spare = lax.dynamic_index_in_dim(v_now, b_now, 0)
+        ledger = []
+        jj = 0
+        while jj < q_next:
+            ledger.append((jj, (jj + k0) % q_next))
+            jj = jj + 1
+        piece_now = lax.ppermute(spare, axis_id, ledger)
+        value_now = lax.dynamic_update_slice_in_dim(value_now, piece_now, carry_out, axis=0)
+        k0 += 1
+    p_next = get_links_by_axis(value_now, view)
+    return p_next
 
 
 def partner(block, axis, bit):
@@ -124,7 +162,7 @@
     kept = lax.dynamic_slice_in_dim(cold_part, myself * half_width, half_width, 1)
     given = lax.dynamic_slice_in_dim(cold_part, (1 - myself) * half_width, half_width, 1)
     owner_sum = kept + partner(given, "heads", 0)
-    returned = lax.all_to_all(owner_sum, "rows", split_axis=0, concat_axis=0, tiled=True)
+    returned = convert_modes_all("rows", 0, owner_sum, 0)
     cold_sum = collect_rows(selector_wide, returned)
     hot_kept = lax.dynamic_slice_in_dim(hot_part, myself * half_width, half_width, 1)
     hot_given = lax.dynamic_slice_in_dim(hot_part, (1 - myself) * half_width, half_width, 1)

time: 45.6 us -> 50.8 us (1.11)
  starting transfers between devices: 11.7 us -> 16 us
  local copies, waits for them, and re-layouts: 3.33 us -> 5.36 us
  other arithmetic: 2.53 us -> 1.58 us
    ppermute x0 -> x7, waiting for transfers between devices: none -> 9.54 us  [convert_modes_all(): piece_now = lax.ppermute(spare, axis_id, ledger)]
    all_to_all x1 -> x0, waiting for transfers between devices: 9.17 us -> none  [local(): lax.all_to_all(owner_sum, 'rows', split_axis=0, concat_axis=0, tiled=True)]
    ppermute x0 -> x7, starting transfers between devices: none -> 7.84 us  [convert_modes_all(): piece_now = lax.ppermute(spare, axis_id, ledger)]
    all_to_all x1 -> x0, starting transfers between devices: 3.59 us -> none  [local(): lax.all_to_all(owner_sum, 'rows', split_axis=0, concat_axis=0, tiled=True)]
    unnamed x20 -> x26, local copies, waits for them, and re-layouts: 1.24 us -> 3.85 us
    ppermute x4, waiting for transfers between devices: 2.3 us -> 1.19 us  [partner(): return lax.ppermute(block, axis, route)]
    all_to_all x2 -> x0, local copies, waits for them, and re-layouts: 1.04 us -> none  [local(): lax.all_to_all(owner_sum, 'rows', split_axis=0, concat_axis=0, tiled=True)]
    add x1, other arithmetic: 0.98 us -> 0.03 us  [local(): owner_sum = kept + partner(given, 'heads', 0)]
  transfers between devices with their start and end apart: 6 -> 12, of which waited for: 5 -> 7; matrix products, arithmetic and copies ran while one was open for 3% -> 3% of each run, Pallas kernels for 0% -> 0%
where the time goes in v1:
time: 50.8 us; the launch traced here: 50.3 us
  waiting for transfers between devices  20.1 us (40%)
  starting transfers between devices  16 us (31%)
  matrix products  6.79 us (13%)
  local copies, waits for them, and re-layouts  5.36 us (11%)
  other arithmetic  1.58 us (3%)
    ppermute x7, waiting for transfers between devices, convert_modes_all(): piece_now = lax.ppermute(spare, axis_id, ledger)  9.54 us
    all_to_all x1, waiting for transfers between devices, local(): lax.all_to_all(outgoing, 'rows', split_axis=0, concat_axis=0, tiled=True)  9.36 us
    ppermute x7, starting transfers between devices, convert_modes_all(): piece_now = lax.ppermute(spare, axis_id, ledger)  7.84 us
    all_to_all x1, starting transfers between devices, local(): lax.all_to_all(outgoing, 'rows', split_axis=0, concat_axis=0, tiled=True)  7.17 us
    unnamed x26, local copies, waits for them, and re-layouts  3.85 us
    dot_general x2, matrix products, swiglu_rows(): return jnp.dot(hidden, down_rows, preferred_element_type=jnp.float32)  2.6 us
    ppermute x4, waiting for transfers between devices, partner(): return lax.ppermute(block, axis, route)  1.19 us
    dot_general x1, matrix products, attention_rows(): jnp.einsum('rgjd,rgpd->rgjp', queries, key_cache, preferred_element_type=...  1.17 us
  transfers between devices with their start and end apart: 12, of which 7 were waited for; matrix products, arithmetic and copies ran while one was open for 3% of the time, Pallas kernels for 0%

profile of v1, /device:TPU:0, one launch (start us, length us, event | category | flops | bytes accessed | tf_op | source)
XLA Modules:
  0.0 50.3 jit_solution(10169091310900609631)
XLA Ops:
  0.0 0.8 %iota_compare_fusion = pred[8,32]{1,0:T(8,128)(4,1)S(1)} fusion(s32[8]{0:T(128)} %param.21), kind=kLoop, calls=%fused_computation.60 | loop fusion | flops 256 | bytes 288 | tf_op jit(solution)/shard_map/lt | solution.py:79
  0.8 1.0 %fusion.14 = f32[8,2,1,16]{3,2,1,0:T(1,128)S(1)} fusion(bf16[8,2,16,128]{3,0,2,1:T(8,128)(2,1)} %bitcast.29, bf16[8,2,128,1]{2,1,0,3:T(2,128)(2,1)} %bitcast.37), kind=kOutput, calls=%fused_computation.26 | convolution fusion | flops 65536 | bytes 70656 | tf_op jit(solution)/shard_map/rgjd,rgd->rgj/dot_general | solution.py:76
  1.8 1.2 %fusion.36 = (f32[8,2,16]{2,1,0:T(2,128)S(1)}, f32[8,2,16,32]{3,2,1,0:T(8,128)S(1)}) fusion(bf16[8,2,32,128]{3,2,1,0:T(8,128)(2,1)} %param.17, bf16[8,2,16,128]{3,0,2,1:T(8,128)(2,1)S(1)} %bitcast.30, pred[8,32]{1,0:T(8,128)(4,1)S(1)} %iota_compare_fusion), kind=kOutput, calls=%fused_computation.72 | convolution fusion | flops 2121472 | bytes 230656 | tf_op jit(solution)/shard_map/rgjd,rgpd->rgjp/dot_general | solution.py:72
  3.0 0.2 fusion.9
  3.3 0.7 %copy-done.11 = bf16[8,2,128]{2,1,0:T(2,128)(2,1)S(1)} copy-done((bf16[8,2,128]{2,1,0:T(2,128)(2,1)S(1)}, bf16[8,2,128]{2,1,0:T(2,128)(2,1)}, u32[]{:S(2)}) %copy-start.11) | copy-done | bytes 4120
  4.0 0.3 convolution_add_fusion
  4.2 0.6 %copy-done.8 = bf16[8,4096]{1,0:T(8,128)(2,1)S(1)} copy-done((bf16[8,4096]{1,0:T(8,128)(2,1)S(1)}, bf16[8,4096]{1,0:T(8,128)(2,1)}, u32[]{:S(2)}) %copy-start.8) | copy-done | bytes 65560
  5.0 0.5 %collective-permute-start = (f32[8]{0:T(128)S(1)}, f32[8]{0:T(128)S(1)}, u32[]{:S(2)}, u32[]{:S(2)}) collective-permute-start(f32[8]{0:T(128)S(1)} %get-tuple-element.5), channel_id=1, source_target_pairs={{0,1},{1,0},{2,3},{3,2},{4,5},{5,4},{6,7},{7,6},{8,9},{9,8},{10,11... | collective-permute-start | bytes 104 | tf_op jit(solution)/shard_map/ppermute | solution.py:56
  5.5 0.7 %copy-done.9 = s32[8,4]{0,1:T(4,128)S(1)} copy-done((s32[8,4]{0,1:T(4,128)S(1)}, s32[8,4]{0,1:T(4,128)}, u32[]{:S(2)}) %copy-start.9) | copy-done | bytes 152
  6.5 0.3 collective-permute-start.1
  6.8 1.0 %collective-permute-done.1 = bf16[8,4096]{1,0:T(8,128)(2,1)S(1)} collective-permute-done((bf16[8,4096]{1,0:T(8,128)(2,1)S(1)}, bf16[8,4096]{1,0:T(8,128)(2,1)S(1)}, u32[]{:S(2)}, u32[]{:S(2)}) %collective-permute-start.1) | collective-permute-done | bytes 65568 | tf_op jit(solution)/shard_map/ppermute | solution.py:56
  7.8 0.2 convolution_convert_fusion
  8.0 0.4 copy-done.5
  8.4 0.9 %all_to_all.8 = bf16[8,2,8192]{2,1,0:T(2,128)(2,1)} reshape(bf16[16,8192]{1,0:T(8,128)(2,1)S(1)} %convolution_convert_fusion) | data formatting | bytes 524288 | tf_op jit(solution)/shard_map/all_to_all | solution.py:159
  9.3 7.2 %all-to-all-start = ((bf16[8,2,8192]{2,1,0:T(2,128)(2,1)}), bf16[8,2,8192]{2,1,0:T(2,128)(2,1)S(1)}, u32[]{:S(2)}, u32[]{:S(2)}) async-start(bf16[8,2,8192]{2,1,0:T(2,128)(2,1)} %all_to_all.8), calls=%async_computation | async-start | bytes 524288 | tf_op jit(solution)/shard_map/all_to_all | solution.py:159
  16.5 9.4 %all-to-all-done = bf16[8,2,8192]{2,1,0:T(2,128)(2,1)S(1)} async-done(((bf16[8,2,8192]{2,1,0:T(2,128)(2,1)}), bf16[8,2,8192]{2,1,0:T(2,128)(2,1)S(1)}, u32[]{:S(2)}, u32[]{:S(2)}) %all-to-all-start) | async-done | bytes 262176 | tf_op jit(solution)/shard_map/all_to_all | solution.py:159
  26.0 0.2 fusion.37
  26.2 0.8 %copy-done.3 = bf16[32,8192]{1,0:T(8,128)(2,1)S(1)} copy-done((bf16[32,8192]{1,0:T(8,128)(2,1)S(1)}, bf16[32,8192]{1,0:T(8,128)(2,1)}, u32[]{:S(2)}) %copy-start.3) | copy-done | bytes 524312
  27.0 1.7 %fusion.2 = f32[16,8192]{1,0:T(8,128)S(1)} fusion(bf16[32,8192]{1,0:T(8,128)(2,1)S(1)} %copy-done.3, bf16[16,8192]{1,0:T(8,128)(2,1)S(1)} %all_to_all.10, bf16[32,8192]{1,0:T(8,128)(2,1)} %param.27, f32[16,32]{1,0:T(8,128)S(1)} %fusion.37), kind=kOutput, calls=%fused_computation.6 | convolution fusion | flops 16780288 | bytes 1837056 | tf_op jit(solution)/shard_map/dot_general | solution.py:103
  29.1 0.7 %copy-done.6 = bf16[8,4096]{1,0:T(8,128)(2,1)S(1)} copy-done((bf16[8,4096]{1,0:T(8,128)(2,1)S(1)}, bf16[8,4096]{1,0:T(8,128)(2,1)}, u32[]{:S(2)}) %copy-start.6) | copy-done | bytes 65560
  29.8 0.4 fusion.33
  30.5 1.5 %collective-permute-start.4 = (f32[1,2,4096]{2,1,0:T(2,128)S(1)}, f32[1,2,4096]{2,1,0:T(2,128)S(1)}, u32[]{:S(2)}, u32[]{:S(2)}) collective-permute-start(f32[1,2,4096]{2,1,0:T(2,128)S(1)} %constant_dynamic-slice_fusion.6), channel_id=1, source_target_pairs={{0,2},{2,4},{4,6},{6,8},{8,10},{10,12},{12,14},{14,0},{1,3},{3,5},... | collective-permute-start | bytes 98312 | tf_op jit(solution)/shard_map/ppermute | solution.py:42
  32.0 0.9 %fusion.27 = f32[8,8192]{1,0:T(8,128)S(1)} fusion(bf16[64,8192]{1,0:T(8,128)(2,1)S(1)} %copy-done, f32[8,64]{1,0:T(8,128)S(1)} %fusion.33, bf16[64,8192]{1,0:T(8,128)(2,1)S(1)} %copy-done.2, bf16[8,4096]{1,0:T(8,128)(2,1)S(1)} %copy-done.6, bf16[8,4096]{1,0:T(8,128)(2,1)S(1)} %fusion.5, pred[]{:T(512)S(6)} %eq.31), kind=kOutput, calls=%fused_computation.62 | convolution fusion | flops 17370112 | bytes 2492417 | tf_op jit(solution)/shard_map/dot_general | solution.py:103
  32.9 4.3 %collective-permute-done.4 = f32[1,2,4096]{2,1,0:T(2,128)S(1)} collective-permute-done((f32[1,2,4096]{2,1,0:T(2,128)S(1)}, f32[1,2,4096]{2,1,0:T(2,128)S(1)}, u32[]{:S(2)}, u32[]{:S(2)}) %collective-permute-start.4) | collective-permute-done | bytes 32800 | tf_op jit(solution)/shard_map/ppermute | solution.py:42
  37.5 2.5 %collective-permute-start.7 = (f32[1,2,4096]{2,1,0:T(2,128)S(1)}, f32[1,2,4096]{2,1,0:T(2,128)S(1)}, u32[]{:S(2)}, u32[]{:S(2)}) collective-permute-start(f32[1,2,4096]{2,1,0:T(2,128)S(1)} %get-tuple-element.10), channel_id=1, source_target_pairs={{0,8},{2,10},{4,12},{6,14},{8,0},{10,2},{12,4},{14,6},{1,9},{3,11}... | collective-permute-start | bytes 98312 | tf_op jit(solution)/shard_map/ppermute | solution.py:42
  40.0 1.3 %collective-permute-start.8 = (f32[1,2,4096]{2,1,0:T(2,128)S(1)}, f32[1,2,4096]{2,1,0:T(2,128)S(1)}, u32[]{:S(2)}, u32[]{:S(2)}) collective-permute-start(f32[1,2,4096]{2,1,0:T(2,128)S(1)} %get-tuple-element.9), channel_id=1, source_target_pairs={{0,10},{2,12},{4,14},{6,0},{8,2},{10,4},{12,6},{14,8},{1,11},{3,13... | collective-permute-start | bytes 98312 | tf_op jit(solution)/shard_map/ppermute | solution.py:42
  41.3 2.1 %collective-permute-done.5 = f32[1,2,4096]{2,1,0:T(2,128)S(1)} collective-permute-done((f32[1,2,4096]{2,1,0:T(2,128)S(1)}, f32[1,2,4096]{2,1,0:T(2,128)S(1)}, u32[]{:S(2)}, u32[]{:S(2)}) %collective-permute-start.5) | collective-permute-done | bytes 32800 | tf_op jit(solution)/shard_map/ppermute | solution.py:42
  43.4 1.7 %collective-permute-start.9 = (f32[1,2,4096]{2,1,0:T(2,128)S(1)}, f32[1,2,4096]{2,1,0:T(2,128)S(1)}, u32[]{:S(2)}, u32[]{:S(2)}) collective-permute-start(f32[1,2,4096]{2,1,0:T(2,128)S(1)} %get-tuple-element.8), channel_id=1, source_target_pairs={{0,12},{2,14},{4,0},{6,2},{8,4},{10,6},{12,8},{14,10},{1,13},{3,15... | collective-permute-start | bytes 98312 | tf_op jit(solution)/shard_map/ppermute | solution.py:42
  45.2 0.7 %collective-permute-start.10 = (f32[1,2,4096]{2,1,0:T(2,128)S(1)}, f32[1,2,4096]{2,1,0:T(2,128)S(1)}, u32[]{:S(2)}, u32[]{:S(2)}) collective-permute-start(f32[1,2,4096]{2,1,0:T(2,128)S(1)} %get-tuple-element.7), channel_id=1, source_target_pairs={{0,14},{2,0},{4,2},{6,4},{8,6},{10,8},{12,10},{14,12},{1,15},{3,1}... | collective-permute-start | bytes 98312 | tf_op jit(solution)/shard_map/ppermute | solution.py:42
  45.9 1.9 %collective-permute-done.9 = f32[1,2,4096]{2,1,0:T(2,128)S(1)} collective-permute-done((f32[1,2,4096]{2,1,0:T(2,128)S(1)}, f32[1,2,4096]{2,1,0:T(2,128)S(1)}, u32[]{:S(2)}, u32[]{:S(2)}) %collective-permute-start.9) | collective-permute-done | bytes 32800 | tf_op jit(solution)/shard_map/ppermute | solution.py:42
  47.8 1.3 %collective-permute-done.10 = f32[1,2,4096]{2,1,0:T(2,128)S(1)} collective-permute-done((f32[1,2,4096]{2,1,0:T(2,128)S(1)}, f32[1,2,4096]{2,1,0:T(2,128)S(1)}, u32[]{:S(2)}, u32[]{:S(2)}) %collective-permute-start.10) | collective-permute-done | bytes 32800 | tf_op jit(solution)/shard_map/ppermute | solution.py:42
  49.3 1.0 %fusion.7 = bf16[8,4096]{1,0:T(8,128)(2,1)} fusion(bf16[8,4096]{1,0:T(8,128)(2,1)S(1)} %get-tuple-element.6, f32[8,4096]{1,0:T(8,128)S(1)} %collective-permute-done.2, f32[8,8192]{1,0:T(8,128)S(1)} %fusion.27, s32[]{:T(128)S(6)} %select_n.129, f32[16,8]{1,0:T(8,128)S(1)} %bitcast.31, f32[16,4096]{1,0:T(8,128)S(1)} %reshape.44), kind=kOutput, calls=%fused_computation.15 | convolution fusion | flops 6455296 | bytes 655876 | tf_op jit(solution)/shard_map/dot_general | solution.py:107
  (56 shorter events, 1.7 us)
Async XLA Ops:
  0.0 32.0 %copy-start = (bf16[64,8192]{1,0:T(8,128)(2,1)S(1)}, bf16[64,8192]{1,0:T(8,128)(2,1)}, u32[]{:S(2)}) copy-start(bf16[64,8192]{1,0:T(8,128)(2,1)} %param.25) | copy-start | bytes 3145732
  0.0 1.8 %copy-start.7 = (bf16[8,4096]{1,0:T(8,128)(2,1)S(1)}, bf16[8,4096]{1,0:T(8,128)(2,1)}, u32[]{:S(2)}) copy-start(bf16[8,4096]{1,0:T(8,128)(2,1)} %param.16) | copy-start | bytes 196612
  3.0 1.0 %copy-start.12 = (bf16[8,2,32,128]{3,2,1,0:T(8,128)(2,1)S(1)}, bf16[8,2,32,128]{3,2,1,0:T(8,128)(2,1)}, u32[]{:S(2)}) copy-start(bf16[8,2,32,128]{3,2,1,0:T(8,128)(2,1)} %param.18) | copy-start | bytes 393220
  3.3 0.7 %copy-start.11 = (bf16[8,2,128]{2,1,0:T(2,128)(2,1)S(1)}, bf16[8,2,128]{2,1,0:T(2,128)(2,1)}, u32[]{:S(2)}) copy-start(bf16[8,2,128]{2,1,0:T(2,128)(2,1)} %param.20) | copy-start | bytes 12292
  4.0 0.8 %copy-start.8 = (bf16[8,4096]{1,0:T(8,128)(2,1)S(1)}, bf16[8,4096]{1,0:T(8,128)(2,1)}, u32[]{:S(2)}) copy-start(bf16[8,4096]{1,0:T(8,128)(2,1)} %param.15) | copy-start | bytes 196612
  4.8 1.6 %copy-start.10 = (bf16[8192]{0:T(1024)(128)(2,1)S(1)}, bf16[8192]{0:T(1024)(128)(2,1)}, u32[]{:S(2)}) copy-start(bf16[8192]{0:T(1024)(128)(2,1)} %param.22) | copy-start | bytes 49156
  5.0 1.4 %collective-permute-start = (f32[8]{0:T(128)S(1)}, f32[8]{0:T(128)S(1)}, u32[]{:S(2)}, u32[]{:S(2)}) collective-permute-start(f32[8]{0:T(128)S(1)} %get-tuple-element.5), channel_id=1, source_target_pairs={{0,1},{1,0},{2,3},{3,2},{4,5},{5,4},{6,7},{7,6},{8,9},{9,8},{10,11... | collective-permute-start | bytes 104 | tf_op jit(solution)/shard_map/ppermute | solution.py:56
  5.5 0.7 %copy-start.9 = (s32[8,4]{0,1:T(4,128)S(1)}, s32[8,4]{0,1:T(4,128)}, u32[]{:S(2)}) copy-start(s32[8,4]{0,1:T(4,128)} %param.29) | copy-start | bytes 388
  6.5 1.3 %collective-permute-start.1 = (bf16[8,4096]{1,0:T(8,128)(2,1)S(1)}, bf16[8,4096]{1,0:T(8,128)(2,1)S(1)}, u32[]{:S(2)}, u32[]{:S(2)}) collective-permute-start(bf16[8,4096]{1,0:T(8,128)(2,1)S(1)} %fusion.5), channel_id=1, source_target_pairs={{0,1},{1,0},{2,3},{3,2},{4,5},{5,4},{6,7},{7,6},{8,9},{9,8},{10,11... | collective-permute-start | bytes 196616 | tf_op jit(solution)/shard_map/ppermute | solution.py:56
  7.8 0.6 %copy-start.5 = (bf16[8,4096]{1,0:T(8,128)(2,1)}, bf16[8,4096]{1,0:T(8,128)(2,1)S(1)}, u32[]{:S(2)}) copy-start(bf16[8,4096]{1,0:T(8,128)(2,1)S(1)} %collective-permute-done.1) | copy-start | bytes 196612
  9.3 16.6 %copy-start.4 = (bf16[32,8192]{1,0:T(8,128)(2,1)S(1)}, bf16[32,8192]{1,0:T(8,128)(2,1)}, u32[]{:S(2)}) copy-start(bf16[32,8192]{1,0:T(8,128)(2,1)} %param.26) | copy-start | bytes 1572868
  9.3 16.5 %all-to-all-start = ((bf16[8,2,8192]{2,1,0:T(2,128)(2,1)}), bf16[8,2,8192]{2,1,0:T(2,128)(2,1)S(1)}, u32[]{:S(2)}, u32[]{:S(2)}) async-start(bf16[8,2,8192]{2,1,0:T(2,128)(2,1)} %all_to_all.8), calls=%async_computation | async-start | bytes 524288 | tf_op jit(solution)/shard_map/all_to_all | solution.py:159
  26.0 1.0 %copy-start.3 = (bf16[32,8192]{1,0:T(8,128)(2,1)S(1)}, bf16[32,8192]{1,0:T(8,128)(2,1)}, u32[]{:S(2)}) copy-start(bf16[32,8192]{1,0:T(8,128)(2,1)} %param.28) | copy-start | bytes 1572868
  27.0 2.1 %copy-start.1 = (bf16[64,8192]{1,0:T(8,128)(2,1)S(1)}, bf16[64,8192]{1,0:T(8,128)(2,1)}, u32[]{:S(2)}) copy-start(bf16[64,8192]{1,0:T(8,128)(2,1)} %param.24) | copy-start | bytes 3145732
  28.7 1.6 %collective-permute-start.3 = (f32[16,4096]{1,0:T(8,128)S(1)}, f32[16,4096]{1,0:T(8,128)S(1)}, u32[]{:S(2)}, u32[]{:S(2)}) collective-permute-start(f32[16,4096]{1,0:T(8,128)S(1)} %constant_dynamic-slice_fusion.7), channel_id=1, source_target_pairs={{0,1},{1,0},{2,3},{3,2},{4,5},{5,4},{6,7},{7,6},{8,9},{9,8},{10,11... | collective-permute-start | bytes 786440 | tf_op jit(solution)/shard_map/ppermute | solution.py:56
  28.9 0.8 %copy-start.6 = (bf16[8,4096]{1,0:T(8,128)(2,1)S(1)}, bf16[8,4096]{1,0:T(8,128)(2,1)}, u32[]{:S(2)}) copy-start(bf16[8,4096]{1,0:T(8,128)(2,1)} %copy-done.5) | copy-start | bytes 196612
  30.2 1.9 %copy-start.2 = (bf16[64,8192]{1,0:T(8,128)(2,1)S(1)}, bf16[64,8192]{1,0:T(8,128)(2,1)}, u32[]{:S(2)}) copy-start(bf16[64,8192]{1,0:T(8,128)(2,1)} %param.23) | copy-start | bytes 3145732
  30.5 6.7 %collective-permute-start.4 = (f32[1,2,4096]{2,1,0:T(2,128)S(1)}, f32[1,2,4096]{2,1,0:T(2,128)S(1)}, u32[]{:S(2)}, u32[]{:S(2)}) collective-permute-start(f32[1,2,4096]{2,1,0:T(2,128)S(1)} %constant_dynamic-slice_fusion.6), channel_id=1, source_target_pairs={{0,2},{2,4},{4,6},{6,8},{8,10},{10,12},{12,14},{14,0},{1,3},{3,5},... | collective-permute-start | bytes 98312 | tf_op jit(solution)/shard_map/ppermute | solution.py:42
  37.3 6.1 %collective-permute-start.5 = (f32[1,2,4096]{2,1,0:T(2,128)S(1)}, f32[1,2,4096]{2,1,0:T(2,128)S(1)}, u32[]{:S(2)}, u32[]{:S(2)}) collective-permute-start(f32[1,2,4096]{2,1,0:T(2,128)S(1)} %get-tuple-element.12), channel_id=1, source_target_pairs={{0,4},{2,6},{4,8},{6,10},{8,12},{10,14},{12,0},{14,2},{1,5},{3,7},... | collective-permute-start | bytes 98312 | tf_op jit(solution)/shard_map/ppermute | solution.py:42
  37.4 11.9 %collective-permute-start.2 = (f32[8,4096]{1,0:T(8,128)S(1)}, f32[8,4096]{1,0:T(8,128)S(1)}, u32[]{:S(2)}, u32[]{:S(2)}) collective-permute-start(f32[8,4096]{1,0:T(8,128)S(1)} %constant_dynamic-slice_fusion.8), channel_id=1, source_target_pairs={{0,1},{1,0},{2,3},{3,2},{4,5},{5,4},{6,7},{7,6},{8,9},{9,8},{10,11... | collective-permute-start | bytes 393224 | tf_op jit(solution)/shard_map/ppermute | solution.py:56
  37.5 7.7 %collective-permute-start.6 = (f32[1,2,4096]{2,1,0:T(2,128)S(1)}, f32[1,2,4096]{2,1,0:T(2,128)S(1)}, u32[]{:S(2)}, u32[]{:S(2)}) collective-permute-start(f32[1,2,4096]{2,1,0:T(2,128)S(1)} %get-tuple-element.11), channel_id=1, source_target_pairs={{0,6},{2,8},{4,10},{6,12},{8,14},{10,0},{12,2},{14,4},{1,7},{3,9},... | collective-permute-start | bytes 98312 | tf_op jit(solution)/shard_map/ppermute | solution.py:42
  37.5 8.3 %collective-permute-start.7 = (f32[1,2,4096]{2,1,0:T(2,128)S(1)}, f32[1,2,4096]{2,1,0:T(2,128)S(1)}, u32[]{:S(2)}, u32[]{:S(2)}) collective-permute-start(f32[1,2,4096]{2,1,0:T(2,128)S(1)} %get-tuple-element.10), channel_id=1, source_target_pairs={{0,8},{2,10},{4,12},{6,14},{8,0},{10,2},{12,4},{14,6},{1,9},{3,11}... | collective-permute-start | bytes 98312 | tf_op jit(solution)/shard_map/ppermute | solution.py:42
  40.0 5.9 %collective-permute-start.8 = (f32[1,2,4096]{2,1,0:T(2,128)S(1)}, f32[1,2,4096]{2,1,0:T(2,128)S(1)}, u32[]{:S(2)}, u32[]{:S(2)}) collective-permute-start(f32[1,2,4096]{2,1,0:T(2,128)S(1)} %get-tuple-element.9), channel_id=1, source_target_pairs={{0,10},{2,12},{4,14},{6,0},{8,2},{10,4},{12,6},{14,8},{1,11},{3,13... | collective-permute-start | bytes 98312 | tf_op jit(solution)/shard_map/ppermute | solution.py:42
  43.4 4.4 %collective-permute-start.9 = (f32[1,2,4096]{2,1,0:T(2,128)S(1)}, f32[1,2,4096]{2,1,0:T(2,128)S(1)}, u32[]{:S(2)}, u32[]{:S(2)}) collective-permute-start(f32[1,2,4096]{2,1,0:T(2,128)S(1)} %get-tuple-element.8), channel_id=1, source_target_pairs={{0,12},{2,14},{4,0},{6,2},{8,4},{10,6},{12,8},{14,10},{1,13},{3,15... | collective-permute-start | bytes 98312 | tf_op jit(solution)/shard_map/ppermute | solution.py:42
  45.2 4.0 %collective-permute-start.10 = (f32[1,2,4096]{2,1,0:T(2,128)S(1)}, f32[1,2,4096]{2,1,0:T(2,128)S(1)}, u32[]{:S(2)}, u32[]{:S(2)}) collective-permute-start(f32[1,2,4096]{2,1,0:T(2,128)S(1)} %get-tuple-element.7), channel_id=1, source_target_pairs={{0,14},{2,0},{4,2},{6,4},{8,6},{10,8},{12,10},{14,12},{1,15},{3,1}... | collective-permute-start | bytes 98312 | tf_op jit(solution)/shard_map/ppermute | solution.py:42
